TPU v7x, 256 devices: a whole 4x4x8 slice. The times are simulated.
256 devices in a mesh: req: 8 (over z), exp: 8 (over y, core), hid: 4 (over x).
Axes of the slice: x: 4, y: 4, z: 8, core: 2. Of those that a mesh axis runs over, the one named last changes fastest.
Arguments:
- layer_input_rows: bfloat16 [16384, 1536], P(('req', 'exp')), may hold values from -6 to 6
- attention_norm_gain: float32 [1536], replicated
- query_weight: bfloat16 [1536, 1536], P(None, 'hid'), may hold values from -1 to 1
- key_weight: bfloat16 [1536, 512], P(None, 'hid'), may hold values from -1 to 1
- value_weight: bfloat16 [1536, 512], P(None, 'hid'), may hold values from -0.15625 to 0.15625
- attention_output_weight: bfloat16 [1536, 1536], P('hid'), may hold values from -0.15625 to 0.15625
- query_down_factor: bfloat16 [64, 1536, 16], P(('req', 'exp')), may hold values from -0.15625 to 0.15625
- query_up_factor: bfloat16 [64, 16, 1536], P(('req', 'exp')), may hold values from -1.5 to 1.5
- value_down_factor: bfloat16 [64, 1536, 16], P(('req', 'exp')), may hold values from -0.15625 to 0.15625
- value_up_factor: bfloat16 [64, 16, 512], P(('req', 'exp')), may hold values from -1.5 to 1.5
- lengths: int32 [8, 4], P('req'), may hold values from 1 to 1024, 2048 in all within a row
- request_adapter: int32 [8, 4], replicated, may hold values from 0 to 63
- adapter_home_row: int32 [64], replicated, may hold values from 0 to 63, each once
- expert_norm_gain: float32 [1536], replicated, may hold values from 0.4 to 1.6
- routes: int32 [16384, 8], P(('req', 'exp', 'hid')), may hold values from 0 to 39, all different within a row; in each aligned block of 64 rows (0 to 63, 64 to 127, ...) at most 16 rows name the same one
- router_expert_weight: float32 [16384, 8], P(('req', 'exp', 'hid')), may hold values from 0.1 to 0.5
- expert_gate_weight: bfloat16 [40, 1536, 512], P('exp', None, 'hid'), may hold values from -0.15625 to 0.15625
- expert_up_weight: bfloat16 [40, 1536, 512], P('exp', None, 'hid'), may hold values from -0.15625 to 0.15625
- expert_down_weight: bfloat16 [40, 512, 1536], P('exp', 'hid'), may hold values from -0.25 to 0.25
Outputs:
- attn_out: bfloat16 [16384, 1536], P(('req', 'exp', 'hid'))
- expert_out: bfloat16 [16384, 1536], P(('req', 'exp', 'hid'))
Inputs may be any that keep to these rules, and one draw needn't show every extreme that they name: `lengths`: each row sums to 2048; its largest entry is exactly 1024. `adapter_home_row`: each adapter row appears once. `routes`: A row names 8 different experts. In the rows of one device (64 consecutive rows, aligned) no expert is named more than 16 times, a bound that some block reaches in some of them.
All inputs are finite; a program needn't handle non-finite values.
Results may differ from a plain program's by a relative error of at most 0.029.
The roundings to bfloat16 on the way count: a program that leaves them out, or rounds other values in their place, can miss the bound.
Values may be sent and summed in bfloat16 or wider, within the bound.
No kernel may reach another device: no remote copies, remote signals or barrier semaphores. Data moves between devices by JAX's collectives and lax.ppermute only.
A program may use at most 128 MiB of HBM per device.

v0:
```python
import jax
import jax.numpy as jnp
from jax import lax
from jax.sharding import PartitionSpec as P

HEAD_WIDTH = 64
scale_attn = 0.015625
residual_mult = 0.22
norm_eps = 1e-06
rope_base = 10000.0
neg_large = -1e30


def rms_norm(values, norm_gain):
    widened = values.astype(jnp.float32)
    mean_sq = jnp.mean(widened * widened, axis=-1, keepdims=True)
    return (widened * lax.rsqrt(mean_sq + norm_eps) * norm_gain).astype(jnp.bfloat16)


def rotary(heads_in, position):
    half_size = heads_in.shape[-1] // 2
    frequency = rope_base ** (-2.0 * jnp.arange(half_size, dtype=jnp.float32) / heads_in.shape[-1])
    angles = position.astype(jnp.float32)[:, None] * frequency[None, :]
    cosine = jnp.cos(angles)[:, None, :]
    sine_part = jnp.sin(angles)[:, None, :]
    first_half = heads_in[..., :half_size]
    second_half = heads_in[..., half_size:]
    return jnp.concatenate(
        [
            first_half * cosine - second_half * sine_part,
            second_half * cosine + first_half * sine_part,
        ],
        axis=-1,
    )


def request_of(row_ids, group_len):
    request_end = jnp.cumsum(group_len)
    return jnp.sum((row_ids[:, None] >= request_end[None, :]).astype(jnp.int32), axis=1)


def locate(row_ids, group_len):
    request_end = jnp.cumsum(group_len)
    request_start = request_end - group_len
    request = request_of(row_ids, group_len)
    member = request[:, None] == jnp.arange(group_len.shape[0], dtype=jnp.int32)[None, :]
    position = row_ids - jnp.sum(jnp.where(member, request_start[None, :], 0), axis=1)
    return (request, member, position)


def expert_rows(rows_in, expert_gate_weight, expert_up_weight, expert_down_weight):
    gate_act = jnp.einsum(
        "red,edf->ref", rows_in, expert_gate_weight, preferred_element_type=jnp.float32
    )
    upper = jnp.einsum(
        "red,edf->ref", rows_in, expert_up_weight, preferred_element_type=jnp.float32
    )
    hidden = (jax.nn.silu(gate_act) * upper).astype(jnp.bfloat16)
    return jnp.einsum(
        "ref,efd->red", hidden, expert_down_weight, preferred_element_type=jnp.float32
    )


def per_device(
    layer_input_rows,
    attention_norm_gain,
    query_weight,
    key_weight,
    value_weight,
    attention_output_weight,
    query_down_factor,
    query_up_factor,
    value_down_factor,
    value_up_factor,
    lengths,
    request_adapter,
    adapter_home_row,
    expert_norm_gain,
    routes,
    router_expert_weight,
    expert_gate_weight,
    expert_up_weight,
    expert_down_weight,
):
    exp_count = lax.axis_size("exp")
    hid_count = lax.axis_size("hid")
    exp_index = lax.axis_index("exp")
    hid_index = lax.axis_index("hid")
    req_index = lax.axis_index("req")
    query_rows = layer_input_rows.shape[0]
    width = layer_input_rows.shape[1]
    kv_local = key_weight.shape[1] // HEAD_WIDTH
    q_local = query_weight.shape[1] // HEAD_WIDTH
    group_share = q_local // kv_local
    adapter_rank_size = query_down_factor.shape[2]
    requests = lengths.shape[1]
    group_len = lengths[0]
    row_ids = exp_index * query_rows + jnp.arange(query_rows, dtype=jnp.int32)
    request, member, position = locate(row_ids, group_len)
    wanted = lax.dynamic_index_in_dim(request_adapter, req_index, 0, keepdims=False)
    slot_ids = jnp.arange(adapter_home_row.shape[0], dtype=jnp.int32)
    home_of = jnp.sum(
        jnp.where(wanted[:, None] == slot_ids[None, :], adapter_home_row[None, :], 0), axis=1
    )
    pieces = (
        lax.all_gather(query_down_factor, ("req", "exp"), axis=0, tiled=True),
        lax.all_gather(query_up_factor, ("req", "exp"), axis=0, tiled=True),
        lax.all_gather(value_down_factor, ("req", "exp"), axis=0, tiled=True),
        lax.all_gather(value_up_factor, ("req", "exp"), axis=0, tiled=True),
    )
    adapter_bank_rows = jnp.arange(pieces[0].shape[0], dtype=jnp.int32)
    selector = (home_of[:, None] == adapter_bank_rows[None, :]).astype(jnp.bfloat16)
    picked_now = tuple(
        (
            jnp.einsum("jn,nab->jab", selector, piece_in, preferred_element_type=jnp.float32)
            for piece_in in pieces
        )
    )
    chosen = tuple((fresh for fresh in picked_now))
    qa_sel, qb_sel, va_sel, vb_sel = [member_in.astype(jnp.bfloat16) for member_in in chosen]
    normed_rows = rms_norm(layer_input_rows, attention_norm_gain)

    def low_rank_term(a_sel, b_sel, width_cols, offset):
        inner_terms = jnp.einsum(
            "td,jdr->tjr", normed_rows, a_sel, preferred_element_type=jnp.float32
        )
        inner_terms = (
            jnp.where(member[:, :, None], inner_terms, 0.0)
            .reshape(query_rows, requests * adapter_rank_size)
            .astype(jnp.bfloat16)
        )
        right_factor = lax.dynamic_slice_in_dim(b_sel, offset, width_cols, 2).reshape(
            requests * adapter_rank_size, width_cols
        )
        return jnp.dot(inner_terms, right_factor, preferred_element_type=jnp.float32)

    query_cols = q_local * HEAD_WIDTH
    kv_cols = kv_local * HEAD_WIDTH
    query_matrix = jnp.dot(
        normed_rows, query_weight, preferred_element_type=jnp.float32
    ) + low_rank_term(qa_sel, qb_sel, query_cols, hid_index * query_cols)
    query_matrix = rotary(query_matrix.reshape(query_rows, q_local, HEAD_WIDTH), position).astype(
        jnp.bfloat16
    )
    query_matrix = query_matrix.reshape(query_rows, kv_local, group_share, HEAD_WIDTH)
    keys_own = jnp.dot(normed_rows, key_weight, preferred_element_type=jnp.float32)
    keys_own = (
        rotary(keys_own.reshape(query_rows, kv_local, HEAD_WIDTH), position)
        .astype(jnp.bfloat16)
        .reshape(query_rows, kv_cols)
    )
    values_own = jnp.dot(
        normed_rows, value_weight, preferred_element_type=jnp.float32
    ) + low_rank_term(va_sel, vb_sel, kv_cols, hid_index * kv_cols)
    values_own = values_own.astype(jnp.bfloat16)
    running_max = jnp.full((kv_local, group_share, query_rows), neg_large, jnp.float32)
    key_piece = lax.all_gather(keys_own, "exp", axis=0, tiled=True)
    value_piece = lax.all_gather(values_own, "exp", axis=0, tiled=True)
    piece_len = key_piece.shape[0]
    key_ids = jnp.arange(piece_len, dtype=jnp.int32)
    key_request = request_of(key_ids, group_len)
    allowed = (request[:, None] == key_request[None, :]) & (key_ids[None, :] <= row_ids[:, None])
    key_heads = key_piece.reshape(piece_len, kv_local, HEAD_WIDTH)
    value_heads = value_piece.reshape(piece_len, kv_local, HEAD_WIDTH)
    scores = (
        jnp.einsum("qkgh,nkh->kgqn", query_matrix, key_heads, preferred_element_type=jnp.float32)
        * scale_attn
    )
    scores = jnp.where(allowed[None, None], scores, neg_large)
    new_max = jnp.maximum(running_max, jnp.max(scores, axis=-1))
    weights = jnp.where(allowed[None, None], jnp.exp(scores - new_max[..., None]), 0.0)
    running_sum = jnp.sum(weights, axis=-1)
    running_out = jnp.einsum(
        "kgqn,nkh->kgqh",
        weights.astype(jnp.bfloat16),
        value_heads,
        preferred_element_type=jnp.float32,
    )
    running_max, running_sum, running_out = (new_max, running_sum, running_out)
    attended = (running_out / running_sum[..., None]).astype(jnp.bfloat16)
    attended = jnp.transpose(attended, (2, 0, 1, 3)).reshape(query_rows, query_cols)
    tok_rows = query_rows // hid_count
    attn_out = lax.psum_scatter(
        jnp.dot(attended, attention_output_weight, preferred_element_type=jnp.float32).astype(
            jnp.bfloat16
        ),
        "hid",
        scatter_dimension=0,
        tiled=True,
    )
    own_rows = lax.dynamic_slice_in_dim(layer_input_rows, hid_index * tok_rows, tok_rows, 0)
    mixed_rows = own_rows.astype(jnp.float32) + residual_mult * attn_out.astype(jnp.float32)
    normed_moe = rms_norm(mixed_rows, expert_norm_gain)
    local_exp = expert_gate_weight.shape[0]
    expert_count = local_exp * exp_count
    top_count = routes.shape[1]
    capacity = max(2, tok_rows // 4)
    flat_route = routes.reshape(tok_rows * top_count)
    route_hits = (flat_route[:, None] == jnp.arange(expert_count, dtype=jnp.int32)[None, :]).astype(
        jnp.int32
    )
    earlier = jnp.cumsum(route_hits, axis=0) - route_hits
    slot_pos = jnp.sum(earlier * route_hits, axis=1)
    slots = slot_pos * expert_count + flat_route
    slot_table = jnp.arange(capacity * expert_count, dtype=jnp.int32)
    placed = jnp.any(
        slot_table[:, None, None] == slots.reshape(tok_rows, top_count)[None], axis=2
    ).astype(jnp.bfloat16)
    outgoing = jnp.dot(placed, normed_moe, preferred_element_type=jnp.float32).astype(jnp.bfloat16)
    outgoing = outgoing.reshape(capacity, expert_count, width)
    copies = jnp.broadcast_to(
        outgoing.reshape(capacity, exp_count, 1, local_exp, width),
        (capacity, exp_count, hid_count, local_exp, width),
    )
    copies = copies.reshape(capacity, exp_count * hid_count * local_exp, width)
    arrived = lax.all_to_all(copies, ("exp", "hid"), split_axis=1, concat_axis=0, tiled=True)
    partials = expert_rows(
        arrived, expert_gate_weight, expert_up_weight, expert_down_weight
    ).astype(jnp.bfloat16)
    returned = lax.all_to_all(partials, ("exp", "hid"), split_axis=0, concat_axis=1, tiled=True)
    returned = returned.reshape(capacity, exp_count, hid_count, local_exp, width)
    results = jnp.sum(returned.astype(jnp.float32), axis=2).astype(jnp.bfloat16)
    results = results.reshape(capacity * expert_count, width)
    picked = jnp.take(results, slots, axis=0).reshape(tok_rows, top_count, width)
    expert_out = jnp.sum(
        router_expert_weight[:, :, None] * picked.astype(jnp.float32), axis=1
    ).astype(jnp.bfloat16)
    return (attn_out, expert_out)


def solution(mesh):
    in_specs = (
        P(("req", "exp"), None),
        P(),
        P(None, "hid"),
        P(None, "hid"),
        P(None, "hid"),
        P("hid", None),
        P(("req", "exp"), None, None),
        P(("req", "exp"), None, None),
        P(("req", "exp"), None, None),
        P(("req", "exp"), None, None),
        P("req", None),
        P(),
        P(),
        P(),
        P(("req", "exp", "hid"), None),
        P(("req", "exp", "hid"), None),
        P("exp", None, "hid"),
        P("exp", None, "hid"),
        P("exp", "hid", None),
    )
    out_specs = (P(("req", "exp", "hid"), None), P(("req", "exp", "hid"), None))
    return jax.shard_map(
        per_device, mesh=mesh, in_specs=in_specs, out_specs=out_specs, check_vma=False
    )
```

profile of v0, /device:TPU:1, one launch (start us, length us, event | category | flops | bytes accessed | tf_op | source)
XLA Modules:
  0.0 728.0 jit_solution(7659078790844080535)
XLA Ops:
  7.2 0.7 all-gather.11.cloned.1.call-update
  8.0 0.7 all-gather.5.cloned.1.call-update
  8.7 0.7 all-gather.7.cloned.1.call-update
  9.4 0.5 all-gather.9.cloned.1.call-update
  10.0 0.8 reduce-window.10
  10.9 0.9 dynamic-slice_reduce_fusion
  11.7 0.1 convert_reduce_fusion
  11.8 0.8 select_reduce_fusion.1
  12.8 0.7 fusion.63
  13.5 1.4 fusion.19
  14.9 0.2 multiply_cosine_fusion
  15.1 1.7 fusion.82
  16.9 0.5 iota_compare_fusion.5
  17.4 17.2 %all_gather.18 = bf16[2048,128]{0,1:T(8,128)(2,1)} all-gather(bf16[256,128]{0,1:T(8,128)(2,1)S(1)} %bitcast.138), channel_id=1, replica_groups=mesh['req'=8,'exp'=8,'hid'=4] {'exp'}, dimensions={0}, use_global_device_ids=true | all-gather | bytes 589824 | tf_op jit(solution)/shard_map/all_gather | solution.py:157
  34.6 0.5 fusion.18
  35.2 56.6 %all-gather.11.cloned.1.call-done = bf16[64,16,512]{2,1,0:T(8,128)(2,1)} async-done(((bf16[1,16,512]{2,1,0:T(8,128)(2,1)}), bf16[64,16,512]{2,1,0:T(8,128)(2,1)}) %all-gather.11.cloned.1.call-update) | async-done | bytes 1048592 | tf_op jit(solution)/shard_map/all_gather | solution.py:109
  91.8 2.4 fusion.34
  94.2 76.1 %all-gather.5.cloned.1.call-done = bf16[64,1536,16]{1,2,0:T(8,128)(2,1)} async-done(((bf16[1,1536,16]{1,2,0:T(8,128)(2,1)}), bf16[64,1536,16]{1,2,0:T(8,128)(2,1)}) %all-gather.5.cloned.1.call-update) | async-done | bytes 3145744 | tf_op jit(solution)/shard_map/all_gather | solution.py:106
  170.3 5.3 fusion.12
  175.6 72.9 %all-gather.7.cloned.1.call-done = bf16[64,16,1536]{2,1,0:T(8,128)(2,1)} async-done(((bf16[1,16,1536]{2,1,0:T(8,128)(2,1)}), bf16[64,16,1536]{2,1,0:T(8,128)(2,1)}) %all-gather.7.cloned.1.call-update) | async-done | bytes 3145744 | tf_op jit(solution)/shard_map/all_gather | solution.py:107
  248.5 5.4 fusion.8
  254.0 0.4 fusion.79
  254.4 0.2 convolution_bitcast_fusion.2
  254.7 1.4 convolution_add_fusion
  256.1 1.9 copy.89
  258.0 1.1 subtract_convert_fusion
  259.1 7.7 %fusion = (f32[2,3,256]{2,1,0:T(4,128)S(1)}, f32[2,2048,256,3]{2,1,3,0:T(8,128)}) fusion(pred[256,2048]{0,1:T(8,128)(4,1)S(1)} %fusion.18, bf16[2048,2,64,1]{0,2,3,1:T(8,128)(2,1)} %bitcast.136, bf16[256,2,3,32]{0,3,2,1:T(8,128)(2,1)S(1)} %bitcast.144, bf16[256,2,3,32]{0,3,2,1:T(8,128)(2,1)S(1)} %bitcast.143), kind=kOutput, calls=%fused_computation.3 | convolution fusion | flops 412482048 | bytes 13834240 | tf_op jit(solution)/shard_map/qkgh,nkh->kgqn/dot_general | solution.py:166
  266.7 0.6 broadcast_maximum_fusion
  267.3 59.3 %all-gather.9.cloned.1.call-done = bf16[64,1536,16]{1,2,0:T(8,128)(2,1)} async-done(((bf16[1,1536,16]{1,2,0:T(8,128)(2,1)}), bf16[64,1536,16]{1,2,0:T(8,128)(2,1)}) %all-gather.9.cloned.1.call-update) | async-done | bytes 3145744 | tf_op jit(solution)/shard_map/all_gather | solution.py:108
  326.6 5.8 fusion.15
  332.5 0.4 fusion.76
  332.9 0.2 convolution_bitcast_fusion.3
  333.1 0.4 fusion.33
  333.6 13.2 %all_gather.23 = bf16[2048,128]{1,0:T(8,128)(2,1)S(1)} all-gather(bf16[256,128]{1,0:T(8,128)(2,1)S(1)} %fusion.33), channel_id=1, replica_groups=mesh['req'=8,'exp'=8,'hid'=4] {'exp'}, dimensions={0}, use_global_device_ids=true | all-gather | bytes 589824 | tf_op jit(solution)/shard_map/all_gather | solution.py:158
  346.8 0.2 copy.94
  347.0 7.5 %fusion.1 = f32[2,3,256]{2,1,0:T(4,128)S(1)} fusion(f32[2,2048,256,3]{2,1,3,0:T(8,128)} %get-tuple-element.11, f32[2,3,256]{2,1,0:T(4,128)} %broadcast_maximum_fusion, pred[256,2048]{0,1:T(8,128)(4,1)S(1)} %fusion.18), kind=kLoop, calls=%fused_computation.4 | loop fusion | flops 15727104 | bytes 13119488 | tf_op jit(solution)/shard_map/reduce_sum | solution.py:172
  354.5 0.7 copy-done.2
  355.3 3.6 fusion.39
  358.9 1.5 convolution_convert_fusion.1
  360.5 0.1 eq.117
  360.7 1.2 reduce-window.11
  361.9 0.2 slice_reduce_fusion
  362.1 0.1 fusion.53
  362.5 0.5 fusion.29
  363.0 17.3 %reduce-scatter.2.cloned.1.call-done = bf16[64,1536]{1,0:T(8,128)(2,1)} async-done(((bf16[256,1536]{1,0:T(8,128)(2,1)}), bf16[64,1536]{1,0:T(8,128)(2,1)}) %reduce-scatter.2.cloned.1.call-update) | async-done | bytes 196624 | tf_op jit(solution)/shard_map/reduce_scatter | solution.py:183
  380.3 1.1 multiply_reduce_fusion.1
  381.5 3.0 convolution_convert_fusion
  384.4 4.3 broadcast_in_dim.129
  388.7 3.2 copy.103
  391.9 1.0 broadcast_in_dim.130
  392.8 98.3 %all_to_all.33 = bf16[16,160,1536]{2,0,1:T(8,128)(2,1)S(1)} all-to-all(bf16[16,160,1536]{2,0,1:T(8,128)(2,1)S(1)} %bitcast.131), channel_id=1, replica_groups=mesh['req'=8,'exp'=8,'hid'=4] {'exp','hid'}, dimensions={1} | all-to-all | bytes 15728640 | tf_op jit(solution)/shard_map/all_to_all | solution.py:216
  491.1 3.9 copy.104
  495.0 6.0 convolution_bitcast_fusion.1
  501.0 12.2 %convert_bitcast_fusion = bf16[512,5,1536]{2,0,1:T(8,128)(2,1)} fusion(bf16[5,128,1536]{2,1,0:T(8,128)(2,1)S(1)} %copy-done, bf16[512,5,1536]{2,0,1:T(8,128)(2,1)} %bitcast.134, bf16[5,1536,128]{2,1,0:T(8,128)(2,1)} %param.36, f32[512,5,128]{2,0,1:T(8,128)S(1)} %convolution_bitcast_fusion.1), kind=kOutput, calls=%fused_computation.6 | convolution fusion | flops 2019164160 | bytes 20971520 | tf_op jit(solution)/shard_map/ref,efd->red/dot_general | solution.py:59
  513.2 12.0 %copy.105 = bf16[512,5,1536]{2,1,0:T(8,128)(2,1)} copy(bf16[512,5,1536]{2,0,1:T(8,128)(2,1)} %convert_bitcast_fusion) | data formatting | bytes 15728640 | tf_op jit(solution)/shard_map/convert_element_type | solution.py:219
  525.1 5.6 all-to-all-start.1
  530.8 0.1 copy.101
  530.9 0.7 copy.96
  531.6 162.9 %all-to-all-done.1 = bf16[512,5,1536]{2,1,0:T(8,128)(2,1)} async-done(((bf16[512,5,1536]{2,1,0:T(8,128)(2,1)}), bf16[512,5,1536]{2,1,0:T(8,128)(2,1)}, u32[]{:S(2)}, u32[]{:S(2)}) %all-to-all-start.1) | async-done | bytes 7864352 | tf_op jit(solution)/shard_map/all_to_all | solution.py:220
  694.5 10.2 %reduce.1 = bf16[16,8,5,1536]{3,2,0,1:T(8,128)(2,1)} reduce(bf16[16,8,4,5,1536]{4,3,0,2,1:T(8,128)(2,1)} %bitcast.39, bf16[]{:T(256)} %constant.89.clone.1), dimensions={2}, to_apply=%region_14.15 | reduce | flops 2949120 | bytes 9830402 | tf_op jit(solution)/shard_map/reduce_sum | solution.py:222
  704.7 3.9 copy.107
  708.6 4.3 reshape.289
  712.9 5.5 gather_fusion
  718.4 2.8 multiply_reduce_fusion
  (73 shorter events, 1.2 us)
Async XLA Ops:
  7.2 493.8 %copy-start = (bf16[5,128,1536]{2,1,0:T(8,128)(2,1)S(1)}, bf16[5,128,1536]{2,1,0:T(8,128)(2,1)}, u32[]{:S(2)}) copy-start(bf16[5,128,1536]{2,1,0:T(8,128)(2,1)} %param.37) | copy-start | bytes 5898244
  7.2 84.6 %all-gather.11.cloned.1.call-start = ((), (), s32[]{:S(2)}) async-start(), calls=%async_computation.6 | async-start | bytes 1064960 | tf_op jit(solution)/shard_map/all_gather | solution.py:109
  7.9 162.4 %all-gather.5.cloned.1.call-start = ((), (), s32[]{:S(2)}) async-start(), calls=%async_computation.3 | async-start | bytes 3194880 | tf_op jit(solution)/shard_map/all_gather | solution.py:106
  8.7 239.9 %all-gather.7.cloned.1.call-start = ((), (), s32[]{:S(2)}) async-start(), calls=%async_computation.4 | async-start | bytes 3194880 | tf_op jit(solution)/shard_map/all_gather | solution.py:107
  9.4 317.2 %all-gather.9.cloned.1.call-start = ((), (), s32[]{:S(2)}) async-start(), calls=%async_computation.5 | async-start | bytes 3194880 | tf_op jit(solution)/shard_map/all_gather | solution.py:108
  10.0 370.3 %reduce-scatter.2.cloned.1.call-start = ((), (), s32[]{:S(2)}) async-start(), calls=%async_computation.7 | async-start | bytes 983040 | tf_op jit(solution)/shard_map/reduce_scatter | solution.py:183
  12.7 157.6 %copy-start.9 = (s32[4]{0:T(128)}, s32[4]{0:T(128)S(1)}, u32[]{:S(2)}) copy-start(s32[4]{0:T(128)S(1)} %select_reduce_fusion.1) | copy-start | bytes 52
  14.9 20.3 %copy-start.14 = (f32[256]{0:T(256)}, f32[256]{0:T(256)S(1)}, u32[]{:S(2)}) copy-start(f32[256]{0:T(256)S(1)} %add_rsqrt_fusion) | copy-start | bytes 3076
  175.6 78.3 %copy-start.3 = (bf16[256,1536]{1,0:T(8,128)(2,1)S(1)}, bf16[256,1536]{1,0:T(8,128)(2,1)}, u32[]{:S(2)}) copy-start(bf16[256,1536]{1,0:T(8,128)(2,1)} %param.19) | copy-start | bytes 2359300
  248.5 5.4 copy-start.15
  248.5 5.5 copy-start.19
  248.5 5.9 copy-start.11
  248.5 6.1 copy-start.17
  259.0 67.5 %copy-start.10 = (s32[4]{0:T(128)S(1)}, s32[4]{0:T(128)}, u32[]{:S(2)}) copy-start(s32[4]{0:T(128)} %copy-done.9) | copy-start | bytes 52
  266.7 65.7 %copy-start.16 = (f32[256]{0:T(256)S(1)}, f32[256]{0:T(256)}, u32[]{:S(2)}) copy-start(f32[256]{0:T(256)} %copy-done.14) | copy-start | bytes 3076
  266.7 65.7 %copy-start.20 = (f32[1536]{0:T(1024)S(1)}, f32[1536]{0:T(1024)}, u32[]{:S(2)}) copy-start(f32[1536]{0:T(1024)} %param.20) | copy-start | bytes 18436
  267.3 65.6 %copy-start.12 = (pred[256,4]{0,1:T(4,128)(4,1)S(1)}, pred[256,4]{0,1:T(4,128)(4,1)}, u32[]{:S(2)}) copy-start(pred[256,4]{0,1:T(4,128)(4,1)} %iota_compare_fusion.5) | copy-start | bytes 3076
  326.6 6.5 copy-start.18
  347.0 8.2 %copy-start.2 = (f32[2,2048,256,3]{2,1,3,0:T(8,128)S(1)}, f32[2,2048,256,3]{2,1,3,0:T(8,128)}, u32[]{:S(2)}) copy-start(f32[2,2048,256,3]{2,1,3,0:T(8,128)} %get-tuple-element.11) | copy-start | bytes 37748740
  347.0 8.2 %copy-start.6 = (f32[2,3,256]{2,1,0:T(4,128)S(1)}, f32[2,3,256]{2,1,0:T(4,128)}, u32[]{:S(2)}) copy-start(f32[2,3,256]{2,1,0:T(4,128)} %broadcast_maximum_fusion) | copy-start | bytes 18436
  355.2 3.6 copy-start.5
  358.9 1.5 copy-start.7
  358.9 21.5 %copy-start.4 = (bf16[256,1536]{1,0:T(8,128)(2,1)S(1)}, bf16[256,1536]{1,0:T(8,128)(2,1)}, u32[]{:S(2)}) copy-start(bf16[256,1536]{1,0:T(8,128)(2,1)} %param.19) | copy-start | bytes 2359300
  358.9 22.6 %copy-start.8 = (f32[1536]{0:T(1024)S(1)}, f32[1536]{0:T(1024)}, u32[]{:S(2)}) copy-start(f32[1536]{0:T(1024)} %param.32) | copy-start | bytes 18436
  525.1 5.8 copy-start.13
  525.1 169.4 %all-to-all-start.1 = ((bf16[512,5,1536]{2,1,0:T(8,128)(2,1)}), bf16[512,5,1536]{2,1,0:T(8,128)(2,1)}, u32[]{:S(2)}, u32[]{:S(2)}) async-start(bf16[512,5,1536]{2,1,0:T(8,128)(2,1)} %copy.105), calls=%async_computation.2 | async-start | bytes 25165824 | tf_op jit(solution)/shard_map/all_to_all | solution.py:220
  712.9 8.3 %copy-start.1 = (bf16[5,128,1536]{2,1,0:T(8,128)(2,1)S(1)}, bf16[5,128,1536]{2,1,0:T(8,128)(2,1)}, u32[]{:S(2)}) copy-start(bf16[5,128,1536]{2,1,0:T(8,128)(2,1)} %param.37) | copy-start | bytes 5898244
Sparse Core Ops, SparseCore 0:
  10.8 80.9 all-gather.10
  94.6 75.7 all-gather.4
  173.1 75.4 all-gather.6
  251.1 75.4 all-gather.8
  360.5 19.7 reduce-scatter.1
where the time goes:
time: 739 us; the launch traced here: 728 us
  waiting for transfers between devices  448 us (61%)
  blocking collectives  129 us (17%)
  matrix products  57.6 us (8%)
  local copies, waits for them, and re-layouts  43.5 us (6%)
  other arithmetic  30.3 us (4%)
  between operations  14.4 us (2%)
    all_to_all x1, waiting for transfers between devices, per_device(): lax.all_to_all(partials, ('exp', 'hid'), split_axis=0, concat_axis=1, til...  163 us
    all_to_all x1, blocking collectives, per_device(): lax.all_to_all(copies, ('exp', 'hid'), split_axis=1, concat_axis=0, tiled...  98.3 us
    all_gather x1, waiting for transfers between devices, per_device(): lax.all_gather(query_down_factor, ('req', 'exp'), axis=0, tiled=True)  76.1 us
    all_gather x1, waiting for transfers between devices, per_device(): lax.all_gather(query_up_factor, ('req', 'exp'), axis=0, tiled=True)  72.9 us
    all_gather x1, waiting for transfers between devices, per_device(): lax.all_gather(value_down_factor, ('req', 'exp'), axis=0, tiled=True)  59.3 us
    all_gather x1, waiting for transfers between devices, per_device(): lax.all_gather(value_up_factor, ('req', 'exp'), axis=0, tiled=True)  56.6 us
    dot_general x4, matrix products, per_device(): jnp.einsum('jn,nab->jab', selector, piece_in, preferred_element_type=jnp....  18.9 us
    reduce_scatter x1, waiting for transfers between devices, per_device(): lax.psum_scatter(jnp.dot(attended, attention_output_weight, preferred_ele...  17.3 us
  transfers between devices with their start and end apart: 6, of which 6 were waited for; matrix products, arithmetic and copies ran while one was open for 5% of the time, Pallas kernels for 0%

commit v1 on v0

--- a/solution.py
+++ b/solution.py
@@ -105,7 +105,12 @@
     pieces = (
         lax.all_gather(query_down_factor, ("req", "exp"), axis=0, tiled=True),
         lax.all_gather(query_up_factor, ("req", "exp"), axis=0, tiled=True),
-        lax.all_gather(value_down_factor, ("req", "exp"), axis=0, tiled=True),
+        jnp.concatenate(
+            lax.all_to_all(
+                jnp.stack([value_down_factor] * lax.axis_size(("req", "exp"))), ("req", "exp"), 0, 0
+            ),
+            axis=0,
+        ),
         lax.all_gather(value_up_factor, ("req", "exp"), axis=0, tiled=True),
     )
     adapter_bank_rows = jnp.arange(pieces[0].shape[0], dtype=jnp.int32)

time: 739 us -> 681 us (0.922)
  waiting for transfers between devices: 448 us -> 384 us
  starting transfers between devices: 5.79 us -> 19.2 us
    all_gather x1 -> x0, waiting for transfers between devices: 59.3 us -> none  [per_device(): lax.all_gather(value_down_factor, ('req', 'exp'), axis=0, tiled=True)]
    all_to_all x0 -> x1, starting transfers between devices: none -> 13.5 us  [per_device(): lax.all_to_all(jnp.stack([value_down_factor] * lax.axis_size(('req', 'exp...]
  transfers between devices with their start and end apart: 6 -> 6, of which waited for: 6 -> 5; matrix products, arithmetic and copies ran while one was open for 5% -> 5% of each run, Pallas kernels for 0% -> 0%
where the time goes in v1:
time: 681 us; the launch traced here: 677 us
  waiting for transfers between devices  384 us (56%)
  blocking collectives  130 us (19%)
  matrix products  56.4 us (8%)
  local copies, waits for them, and re-layouts  45.5 us (7%)
  other arithmetic  27.6 us (4%)
  starting transfers between devices  19.2 us (3%)
  between operations  14.4 us (2%)
    all_to_all x1, waiting for transfers between devices, per_device(): lax.all_to_all(partials, ('exp', 'hid'), split_axis=0, concat_axis=1, til...  163 us
    all_to_all x1, blocking collectives, per_device(): lax.all_to_all(copies, ('exp', 'hid'), split_axis=1, concat_axis=0, tiled...  98.3 us
    all_gather x1, waiting for transfers between devices, per_device(): lax.all_gather(query_down_factor, ('req', 'exp'), axis=0, tiled=True)  76.1 us
    all_gather x1, waiting for transfers between devices, per_device(): lax.all_gather(query_up_factor, ('req', 'exp'), axis=0, tiled=True)  72.9 us
    all_gather x1, waiting for transfers between devices, per_device(): lax.all_gather(value_up_factor, ('req', 'exp'), axis=0, tiled=True)  52.7 us
    dot_general x4, matrix products, per_device(): jnp.einsum('jn,nab->jab', selector, piece_in, preferred_element_type=jnp....  19 us
    all_gather x1, blocking collectives, per_device(): key_piece = lax.all_gather(keys_own, 'exp', axis=0, tiled=True)  18 us
    reduce_scatter x1, waiting for transfers between devices, per_device(): lax.psum_scatter(jnp.dot(attended, attention_output_weight, preferred_ele...  17.3 us
  transfers between devices with their start and end apart: 6, of which 5 were waited for; matrix products, arithmetic and copies ran while one was open for 5% of the time, Pallas kernels for 0%

profile of v1, /device:TPU:1, one launch (start us, length us, event | category | flops | bytes accessed | tf_op | source)
XLA Modules:
  0.0 676.7 jit_solution(16038844144792659392)
XLA Ops:
  7.2 0.7 all-gather.8.cloned.1.call-update
  8.0 0.7 all-gather.4.cloned.1.call-update
  8.7 0.7 all-gather.6.cloned.1.call-update
  9.4 2.8 stack.2
  12.3 13.5 %all-to-all-start = ((bf16[64,1,1536,16]{2,3,1,0:T(8,128)(2,1)}), bf16[64,1,1536,16]{2,3,1,0:T(8,128)(2,1)}, u32[]{:S(2)}, u32[]{:S(2)}) async-start(bf16[64,1,1536,16]{2,3,1,0:T(8,128)(2,1)} %stack.2), calls=%async_computation | async-start | bytes 6291456 | tf_op jit(solution)/shard_map/all_to_all | solution.py:109
  25.8 0.2 reduce-window.10
  26.0 0.2 dynamic-slice_reduce_fusion
  26.2 0.1 convert_reduce_fusion
  26.3 0.2 select_reduce_fusion.1
  26.7 0.2 fusion.20
  26.9 0.2 multiply_cosine_fusion
  27.1 0.5 fusion.83
  27.7 0.6 iota_compare_fusion.5
  28.3 18.0 %all_gather.15 = bf16[2048,128]{0,1:T(8,128)(2,1)} all-gather(bf16[256,128]{0,1:T(8,128)(2,1)S(1)} %bitcast.144), channel_id=1, replica_groups=mesh['req'=8,'exp'=8,'hid'=4] {'exp'}, dimensions={0}, use_global_device_ids=true | all-gather | bytes 589824 | tf_op jit(solution)/shard_map/all_gather | solution.py:162
  46.3 0.8 fusion.19
  47.1 52.7 %all-gather.8.cloned.1.call-done = bf16[64,16,512]{2,1,0:T(8,128)(2,1)} async-done(((bf16[1,16,512]{2,1,0:T(8,128)(2,1)}), bf16[64,16,512]{2,1,0:T(8,128)(2,1)}) %all-gather.8.cloned.1.call-update) | async-done | bytes 1048592 | tf_op jit(solution)/shard_map/all_gather | solution.py:114
  99.8 2.4 fusion.35
  102.2 76.1 %all-gather.4.cloned.1.call-done = bf16[64,1536,16]{1,2,0:T(8,128)(2,1)} async-done(((bf16[1,1536,16]{1,2,0:T(8,128)(2,1)}), bf16[64,1536,16]{1,2,0:T(8,128)(2,1)}) %all-gather.4.cloned.1.call-update) | async-done | bytes 3145744 | tf_op jit(solution)/shard_map/all_gather | solution.py:106
  178.4 5.3 fusion.13
  183.7 72.9 %all-gather.6.cloned.1.call-done = bf16[64,16,1536]{2,1,0:T(8,128)(2,1)} async-done(((bf16[1,16,1536]{2,1,0:T(8,128)(2,1)}), bf16[64,16,1536]{2,1,0:T(8,128)(2,1)}) %all-gather.6.cloned.1.call-update) | async-done | bytes 3145744 | tf_op jit(solution)/shard_map/all_gather | solution.py:107
  256.6 5.4 fusion.9
  262.0 0.4 fusion.80
  262.5 0.2 convolution_bitcast_fusion.2
  262.7 1.4 convolution_add_fusion
  264.1 1.9 copy.91
  266.0 1.1 subtract_convert_fusion
  267.1 7.7 %fusion = (f32[2,3,256]{2,1,0:T(4,128)S(1)}, f32[2,2048,256,3]{2,1,3,0:T(8,128)}) fusion(pred[256,2048]{0,1:T(8,128)(4,1)S(1)} %fusion.19, bf16[2048,2,64,1]{0,2,3,1:T(8,128)(2,1)} %bitcast.142, bf16[256,2,3,32]{0,3,2,1:T(8,128)(2,1)S(1)} %bitcast.150, bf16[256,2,3,32]{0,3,2,1:T(8,128)(2,1)S(1)} %bitcast.149), kind=kOutput, calls=%fused_computation.3 | convolution fusion | flops 412482048 | bytes 13834240 | tf_op jit(solution)/shard_map/qkgh,nkh->kgqn/dot_general | solution.py:171
  274.8 0.6 broadcast_maximum_fusion
  275.4 5.9 fusion.16
  281.3 0.4 fusion.77
  281.8 0.2 convolution_bitcast_fusion.3
  282.0 0.4 fusion.34
  282.4 13.2 %all_gather.19 = bf16[2048,128]{1,0:T(8,128)(2,1)S(1)} all-gather(bf16[256,128]{1,0:T(8,128)(2,1)S(1)} %fusion.34), channel_id=1, replica_groups=mesh['req'=8,'exp'=8,'hid'=4] {'exp'}, dimensions={0}, use_global_device_ids=true | all-gather | bytes 589824 | tf_op jit(solution)/shard_map/all_gather | solution.py:163
  295.6 0.2 copy.96
  295.9 7.5 %fusion.1 = f32[2,3,256]{2,1,0:T(4,128)S(1)} fusion(f32[2,2048,256,3]{2,1,3,0:T(8,128)} %get-tuple-element.11, f32[2,3,256]{2,1,0:T(4,128)} %broadcast_maximum_fusion, pred[256,2048]{0,1:T(8,128)(4,1)S(1)} %fusion.19), kind=kLoop, calls=%fused_computation.4 | loop fusion | flops 15727104 | bytes 13119488 | tf_op jit(solution)/shard_map/reduce_sum | solution.py:177
  303.4 0.7 copy-done.1
  304.1 3.6 fusion.40
  307.8 1.5 convolution_convert_fusion.1
  309.4 0.1 eq.117
  309.5 1.2 reduce-window.11
  310.7 0.2 slice_reduce_fusion
  311.0 0.1 fusion.54
  311.4 0.5 fusion.30
  311.9 17.3 %reduce-scatter.2.cloned.1.call-done = bf16[64,1536]{1,0:T(8,128)(2,1)} async-done(((bf16[256,1536]{1,0:T(8,128)(2,1)}), bf16[64,1536]{1,0:T(8,128)(2,1)}) %reduce-scatter.2.cloned.1.call-update) | async-done | bytes 196624 | tf_op jit(solution)/shard_map/reduce_scatter | solution.py:188
  329.2 1.1 multiply_reduce_fusion.1
  330.3 3.0 convolution_convert_fusion
  333.3 4.3 broadcast_in_dim.129
  337.5 3.2 copy.105
  340.7 1.0 broadcast_in_dim.130
  341.7 98.3 %all_to_all.38 = bf16[16,160,1536]{2,0,1:T(8,128)(2,1)S(1)} all-to-all(bf16[16,160,1536]{2,0,1:T(8,128)(2,1)S(1)} %bitcast.137), channel_id=1, replica_groups=mesh['req'=8,'exp'=8,'hid'=4] {'exp','hid'}, dimensions={1} | all-to-all | bytes 15728640 | tf_op jit(solution)/shard_map/all_to_all | solution.py:221
  440.0 3.9 copy.106
  443.8 6.0 convolution_bitcast_fusion.1
  449.8 12.2 %convert_bitcast_fusion = bf16[512,5,1536]{2,0,1:T(8,128)(2,1)} fusion(bf16[5,128,1536]{2,1,0:T(8,128)(2,1)S(1)} %copy-done, bf16[512,5,1536]{2,0,1:T(8,128)(2,1)} %bitcast.140, bf16[5,1536,128]{2,1,0:T(8,128)(2,1)} %param.36, f32[512,5,128]{2,0,1:T(8,128)S(1)} %convolution_bitcast_fusion.1), kind=kOutput, calls=%fused_computation.6 | convolution fusion | flops 2019164160 | bytes 20971520 | tf_op jit(solution)/shard_map/ref,efd->red/dot_general | solution.py:59
  462.0 12.0 %copy.107 = bf16[512,5,1536]{2,1,0:T(8,128)(2,1)} copy(bf16[512,5,1536]{2,0,1:T(8,128)(2,1)} %convert_bitcast_fusion) | data formatting | bytes 15728640 | tf_op jit(solution)/shard_map/convert_element_type | solution.py:224
  474.0 5.6 all-to-all-start.2
  479.6 0.1 reshape.297
  479.7 0.1 copy.103
  479.8 0.7 copy.98
  480.5 162.9 %all-to-all-done.2 = bf16[512,5,1536]{2,1,0:T(8,128)(2,1)} async-done(((bf16[512,5,1536]{2,1,0:T(8,128)(2,1)}), bf16[512,5,1536]{2,1,0:T(8,128)(2,1)}, u32[]{:S(2)}, u32[]{:S(2)}) %all-to-all-start.2) | async-done | bytes 7864352 | tf_op jit(solution)/shard_map/all_to_all | solution.py:225
  643.4 10.2 %reduce.1 = bf16[16,8,5,1536]{3,2,0,1:T(8,128)(2,1)} reduce(bf16[16,8,4,5,1536]{4,3,0,2,1:T(8,128)(2,1)} %bitcast.41, bf16[]{:T(256)} %constant.89.clone.1), dimensions={2}, to_apply=%region_14.15 | reduce | flops 2949120 | bytes 9830402 | tf_op jit(solution)/shard_map/reduce_sum | solution.py:227
  653.5 3.9 copy.109
  657.4 4.3 reshape.296
  661.7 5.4 gather_fusion
  667.1 2.8 multiply_reduce_fusion
  (81 shorter events, 1.1 us)
Async XLA Ops:
  7.2 442.7 %copy-start = (bf16[5,128,1536]{2,1,0:T(8,128)(2,1)S(1)}, bf16[5,128,1536]{2,1,0:T(8,128)(2,1)}, u32[]{:S(2)}) copy-start(bf16[5,128,1536]{2,1,0:T(8,128)(2,1)} %param.37) | copy-start | bytes 5898244
  7.2 92.6 %all-gather.8.cloned.1.call-start = ((), (), s32[]{:S(2)}) async-start(), calls=%async_computation.6 | async-start | bytes 1064960 | tf_op jit(solution)/shard_map/all_gather | solution.py:114
  7.9 170.5 %all-gather.4.cloned.1.call-start = ((), (), s32[]{:S(2)}) async-start(), calls=%async_computation.4 | async-start | bytes 3194880 | tf_op jit(solution)/shard_map/all_gather | solution.py:106
  8.7 247.9 %all-gather.6.cloned.1.call-start = ((), (), s32[]{:S(2)}) async-start(), calls=%async_computation.5 | async-start | bytes 3194880 | tf_op jit(solution)/shard_map/all_gather | solution.py:107
  12.2 13.6 %copy-start.24 = (s32[1,4]{1,0:T(1,128)S(1)}, s32[1,4]{1,0:T(1,128)}, u32[]{:S(2)}) copy-start(s32[1,4]{1,0:T(1,128)} %param.29) | copy-start | bytes 52
  12.2 13.7 %copy-start.13 = (s32[8,4]{0,1:T(4,128)S(1)}, s32[8,4]{0,1:T(4,128)}, u32[]{:S(2)}) copy-start(s32[8,4]{0,1:T(4,128)} %param.30) | copy-start | bytes 388
  12.2 14.0 %copy-start.23 = (s32[64]{0:T(128)S(1)}, s32[64]{0:T(128)}, u32[]{:S(2)}) copy-start(s32[64]{0:T(128)} %param.31) | copy-start | bytes 772
  12.2 14.4 %copy-start.2 = (bf16[256,1536]{1,0:T(8,128)(2,1)S(1)}, bf16[256,1536]{1,0:T(8,128)(2,1)}, u32[]{:S(2)}) copy-start(bf16[256,1536]{1,0:T(8,128)(2,1)} %param.19) | copy-start | bytes 2359300
  12.2 14.9 %copy-start.18 = (bf16[1536,128]{1,0:T(8,128)(2,1)S(1)}, bf16[1536,128]{1,0:T(8,128)(2,1)}, u32[]{:S(2)}) copy-start(bf16[1536,128]{1,0:T(8,128)(2,1)} %param.22) | copy-start | bytes 1179652
  12.3 14.9 %copy-start.20 = (f32[1536]{0:T(1024)S(1)}, f32[1536]{0:T(1024)}, u32[]{:S(2)}) copy-start(f32[1536]{0:T(1024)} %param.20) | copy-start | bytes 18436
  12.3 263.1 %all-to-all-start = ((bf16[64,1,1536,16]{2,3,1,0:T(8,128)(2,1)}), bf16[64,1,1536,16]{2,3,1,0:T(8,128)(2,1)}, u32[]{:S(2)}, u32[]{:S(2)}) async-start(bf16[64,1,1536,16]{2,3,1,0:T(8,128)(2,1)} %stack.2), calls=%async_computation | async-start | bytes 6291456 | tf_op jit(solution)/shard_map/all_to_all | solution.py:109
  25.7 303.4 %reduce-scatter.2.cloned.1.call-start = ((), (), s32[]{:S(2)}) async-start(), calls=%async_computation.7 | async-start | bytes 983040 | tf_op jit(solution)/shard_map/reduce_scatter | solution.py:188
  26.5 151.9 %copy-start.8 = (s32[4]{0:T(128)}, s32[4]{0:T(128)S(1)}, u32[]{:S(2)}) copy-start(s32[4]{0:T(128)S(1)} %select_reduce_fusion.1) | copy-start | bytes 52
  26.9 19.4 %copy-start.14 = (f32[256]{0:T(256)}, f32[256]{0:T(256)S(1)}, u32[]{:S(2)}) copy-start(f32[256]{0:T(256)S(1)} %add_rsqrt_fusion) | copy-start | bytes 3076
  256.6 5.4 copy-start.15
  256.6 5.4 copy-start.21
  256.6 5.9 copy-start.10
  256.6 6.1 copy-start.17
  267.1 8.3 %copy-start.9 = (s32[4]{0:T(128)S(1)}, s32[4]{0:T(128)}, u32[]{:S(2)}) copy-start(s32[4]{0:T(128)} %copy-done.8) | copy-start | bytes 52
  274.8 6.5 copy-start.16
  274.8 6.5 copy-start.22
  275.4 6.4 copy-start.11
  275.4 6.6 copy-start.19
  295.9 8.2 %copy-start.1 = (f32[2,2048,256,3]{2,1,3,0:T(8,128)S(1)}, f32[2,2048,256,3]{2,1,3,0:T(8,128)}, u32[]{:S(2)}) copy-start(f32[2,2048,256,3]{2,1,3,0:T(8,128)} %get-tuple-element.11) | copy-start | bytes 37748740
  295.9 8.2 %copy-start.5 = (f32[2,3,256]{2,1,0:T(4,128)S(1)}, f32[2,3,256]{2,1,0:T(4,128)}, u32[]{:S(2)}) copy-start(f32[2,3,256]{2,1,0:T(4,128)} %broadcast_maximum_fusion) | copy-start | bytes 18436
  304.1 3.6 copy-start.4
  307.7 1.5 copy-start.6
  307.7 21.5 %copy-start.3 = (bf16[256,1536]{1,0:T(8,128)(2,1)S(1)}, bf16[256,1536]{1,0:T(8,128)(2,1)}, u32[]{:S(2)}) copy-start(bf16[256,1536]{1,0:T(8,128)(2,1)} %param.19) | copy-start | bytes 2359300
  307.7 22.6 %copy-start.7 = (f32[1536]{0:T(1024)S(1)}, f32[1536]{0:T(1024)}, u32[]{:S(2)}) copy-start(f32[1536]{0:T(1024)} %param.32) | copy-start | bytes 18436
  474.0 5.8 copy-start.12
  474.0 169.4 %all-to-all-start.2 = ((bf16[512,5,1536]{2,1,0:T(8,128)(2,1)}), bf16[512,5,1536]{2,1,0:T(8,128)(2,1)}, u32[]{:S(2)}, u32[]{:S(2)}) async-start(bf16[512,5,1536]{2,1,0:T(8,128)(2,1)} %copy.107), calls=%async_computation.3 | async-start | bytes 25165824 | tf_op jit(solution)/shard_map/all_to_all | solution.py:225
Sparse Core Ops, SparseCore 0:
  10.8 88.9 all-gather.7
  102.6 75.7 all-gather.3
  181.1 75.4 all-gather.5
  309.4 19.7 reduce-scatter.1
